TPU v7x, 256 devices: a whole 4x4x8 slice. The times are simulated.
256 devices in a mesh: dp: 8 (over x, core), expert: 16 (over y, z_hi), tensor: 2 (over z_lo).
Axes of the slice: x: 4, y: 4, z: 8 (z_hi: 4, z_lo: 2; z = z_hi * 2 + z_lo), core: 2. Of those that a mesh axis runs over, the one named last changes fastest.
Arguments:
- tokens: bfloat16 [1024, 7168], P(('dp', 'expert'), 'tensor'), may hold values from -6 to 6
- upstream: bfloat16 [1024, 7168], P(('dp', 'expert'), 'tensor'), may hold values from -3 to 3
- probs: bfloat16 [1024, 8], P(('dp', 'expert')), may hold values from 0.049804688 to 0.59765625
- routing: int32 [1024, 8], P(('dp', 'expert')), may hold values from 0 to 15, all different within a row; in each aligned block of 8 rows (0 to 7, 8 to 15, ...) at most 5 rows name the same one
- row_rollout: int32 [1024], P(('dp', 'expert')), may hold values from 0 to 255
- group_ids: int32 [256], replicated, may hold values from 0 to 31
- rewards: int32 [256], replicated, may hold values from 0 to 1
- w_gate: bfloat16 [16, 7168, 2048], P('expert', None, ('dp', 'tensor')), may hold values from -0.0625 to 0.0625
- w_up: bfloat16 [16, 7168, 2048], P('expert', None, ('dp', 'tensor')), may hold values from -0.0625 to 0.0625
- w_down: bfloat16 [16, 2048, 7168], P('expert', ('dp', 'tensor')), may hold values from -0.125 to 0.125
Outputs:
- input_grad: bfloat16 [1024, 7168], P(('dp', 'expert'), 'tensor')
- route_grad: bfloat16 [1024, 8], P(('dp', 'expert'))
- grad_gate: bfloat16 [16, 7168, 2048], P('expert', None, ('dp', 'tensor'))
- grad_up: bfloat16 [16, 7168, 2048], P('expert', None, ('dp', 'tensor'))
- grad_down: bfloat16 [16, 2048, 7168], P('expert', ('dp', 'tensor'))
Inputs may be any that keep to these rules, and one draw needn't show every extreme that they name: `routing`: each row names 8 different experts. Within each aligned block of 8 rows (the tokens of one index pair of dp and expert) no expert is named by more than 5 rows, a bound that some block reaches.
All inputs are finite; a program needn't handle non-finite values.
Results may differ from a plain program's by a relative error of at most 0.025.
Values may be sent and summed in bfloat16 or wider, within the bound.
No kernel may reach another device: no remote copies, remote signals or barrier semaphores. Data moves between devices by JAX's collectives and lax.ppermute only.
A program may use at most 128 MiB of HBM per device.

v0:
```python
import jax
import jax.numpy as jnp
from jax import lax
from jax.sharding import PartitionSpec as P


def advantages(row_rollout, group_ids, rewards):
    same_group = (group_ids[:, None] == group_ids[None, :]).astype(jnp.float32)
    reward_values = rewards.astype(jnp.float32)
    group_total = jnp.dot(same_group, reward_values, precision=lax.Precision.HIGHEST)
    group_count = jnp.sum(same_group, axis=1)
    per_rollout = reward_values - group_total / group_count
    member = (
        row_rollout[:, None] == jnp.arange(per_rollout.shape[0], dtype=jnp.int32)[None, :]
    ).astype(jnp.float32)
    return jnp.dot(member, per_rollout, precision=lax.Precision.HIGHEST)


def selection(routing, probs, experts, capacity):
    route_hits = (
        routing[:, :, None] == jnp.arange(experts, dtype=jnp.int32)[None, None, :]
    ).astype(jnp.float32)
    occupied = jnp.sum(route_hits, axis=1)
    weight = jnp.einsum("rke,rk->re", route_hits, probs.astype(jnp.float32))
    before = jnp.cumsum(occupied, axis=0) - occupied
    slot_index = jnp.arange(capacity, dtype=jnp.float32)
    chosen = occupied.T[:, None, :] * (before.T[:, None, :] == slot_index[None, :, None]).astype(
        jnp.float32
    )
    return (route_hits, weight, chosen)


def shards(tokens, upstream, probs, routing, row_rollout, group_ids, rewards, w_gate, w_up, w_down):
    f32 = jnp.float32
    bf16 = jnp.bfloat16
    experts = lax.axis_size("expert")
    dp_size = lax.axis_size("dp")
    tensor_size = lax.axis_size("tensor")
    group_rows, features = tokens.shape
    routes_per_row = routing.shape[1]
    capacity = min(group_rows, 5 * group_rows * routes_per_row // (4 * experts))
    slots = experts * capacity
    advantage = advantages(row_rollout, group_ids, rewards)
    cotangent = (advantage[:, None] * upstream.astype(f32)).astype(bf16)
    route_hits, weight, chosen = selection(routing, probs, experts, capacity)
    chosen_half = chosen.astype(bf16)
    both = jnp.stack([tokens, cotangent])
    packed = jnp.einsum("ecr,arf->aecf", chosen_half, both, preferred_element_type=f32).astype(bf16)
    packed_prob = jnp.einsum("ecr,re->ec", chosen, weight).astype(bf16)
    prob_row = jnp.zeros((experts, 1, features), bf16).at[:, 0, :capacity].set(packed_prob)
    chunk = slots + 8
    all_rows = dp_size * chunk
    extra = jnp.zeros((chunk - slots, features), bf16)
    tok_pack = jnp.concatenate([packed[0], prob_row], axis=1)
    arrived_tok = lax.all_to_all(tok_pack, "expert", split_axis=0, concat_axis=0, tiled=True)
    extra_prob = extra.at[0, :slots].set(arrived_tok[:, capacity, :capacity].reshape(slots))
    tok_rows = jnp.concatenate([arrived_tok[:, :capacity].reshape(slots, features), extra_prob])
    tok_rows, cot_pack = lax.optimization_barrier((tok_rows, packed[1]))
    arrived_cot = lax.all_to_all(cot_pack, "expert", split_axis=0, concat_axis=0, tiled=True)
    cot_rows = jnp.concatenate([arrived_cot.reshape(slots, features), extra])
    g_tok = lax.all_gather(tok_rows, ("tensor", "dp"), axis=0, tiled=True)
    g_tok = g_tok.reshape(tensor_size, all_rows, features)
    g_cot = lax.all_gather(cot_rows, ("tensor", "dp"), axis=0, tiled=True)
    g_cot = g_cot.reshape(tensor_size, all_rows, features)
    slot_prob = g_tok[0].reshape(dp_size, chunk, features)[:, slots, :chunk].reshape(all_rows)
    wg = w_gate[0].reshape(tensor_size, features, -1)
    wu = w_up[0].reshape(tensor_size, features, -1)
    wd = w_down[0]
    hidden_width = wd.shape[0]
    wd = wd.reshape(hidden_width, tensor_size, features)
    w_in = jnp.concatenate([wg, wu], axis=2)
    gate_up = sum(
        (jnp.dot(g_tok[t], w_in[t], preferred_element_type=f32) for t in range(tensor_size))
    )
    gate = gate_up[:, :hidden_width]
    up_part = gate_up[:, hidden_width:]
    back_hidden = jnp.einsum("tsf,htf->sh", g_cot, wd, preferred_element_type=f32)
    sigmoid_gate = jax.nn.sigmoid(gate)
    active = gate * sigmoid_gate
    hidden = (active * up_part).astype(bf16)
    hidden_wide = lax.optimization_barrier(hidden).astype(f32)
    route_part = jnp.sum(hidden_wide * back_hidden, axis=-1)
    scale = slot_prob.astype(f32)[:, None]
    scaled = scale * back_hidden
    grad_g = (scaled * up_part * sigmoid_gate * (1.0 + gate * (1.0 - sigmoid_gate))).astype(bf16)
    grad_u = (scaled * active).astype(bf16)
    weighted = (scale * hidden_wide).astype(bf16)
    grad_down = jnp.concatenate(
        [
            jnp.dot(weighted.T, g_cot[t], preferred_element_type=f32).astype(bf16)
            for t in range(tensor_size)
        ],
        axis=1,
    )
    grad_gate = jnp.concatenate(
        [
            jnp.dot(g_tok[t].T, grad_g, preferred_element_type=f32).astype(bf16)
            for t in range(tensor_size)
        ],
        axis=0,
    )
    grad_up = jnp.concatenate(
        [
            jnp.dot(g_tok[t].T, grad_u, preferred_element_type=f32).astype(bf16)
            for t in range(tensor_size)
        ],
        axis=0,
    )
    route_hi = route_part.astype(bf16).reshape(dp_size, chunk)
    route_lo = (route_part.reshape(dp_size, chunk) - route_hi.astype(f32)).astype(bf16)
    carry = jnp.zeros((dp_size, chunk, hidden_width), bf16)
    carry = carry.at[:, slots, :chunk].set(route_hi).at[:, slots + 1, :chunk].set(route_lo)
    lhs = jnp.concatenate([grad_g, grad_u, carry.reshape(all_rows, hidden_width)], axis=1)
    eye = (
        lax.broadcasted_iota(jnp.int32, (features, hidden_width), 0)
        == lax.broadcasted_iota(jnp.int32, (features, hidden_width), 1)
    ).astype(bf16)
    w_out = jnp.concatenate([wg, wu, jnp.broadcast_to(eye, wg.shape)], axis=2)
    product = jnp.einsum("sk,tfk->tsf", lhs, w_out, preferred_element_type=f32).astype(bf16)
    product = product.reshape(tensor_size * all_rows, features)
    own_rows = lax.psum_scatter(product, ("tensor", "dp"), scatter_dimension=0, tiled=True)
    own_rows, grad_gate, grad_up, grad_down = lax.optimization_barrier(
        (own_rows, grad_gate, grad_up, grad_down)
    )
    own_route = (
        own_rows[slots, :slots].astype(f32) + own_rows[slots + 1, :slots].astype(f32)
    ).astype(bf16)
    partner = lax.ppermute(own_route, "tensor", [(i, i ^ 1) for i in range(tensor_size)])
    own_route = jnp.where(lax.axis_index("tensor") == 0, own_route, partner)
    route_row = (
        jnp.zeros((experts, 1, features), bf16)
        .at[:, 0, :capacity]
        .set(own_route.reshape(experts, capacity))
    )
    back_pack = jnp.concatenate(
        [own_rows[:slots].reshape(experts, capacity, features), route_row], axis=1
    )
    home = lax.all_to_all(back_pack, "expert", split_axis=0, concat_axis=0, tiled=True)
    input_grad = jnp.einsum(
        "ecr,ecf->rf", chosen_half, home[:, :capacity], preferred_element_type=f32
    ).astype(bf16)
    per_expert = jnp.einsum("ecr,ec->re", chosen, home[:, capacity, :capacity].astype(f32))
    route_grad = jnp.einsum("rke,re->rk", route_hits, per_expert).astype(bf16)
    return (input_grad, route_grad, grad_gate[None], grad_up[None], grad_down[None])


def solution(mesh):
    in_specs = (
        P(("dp", "expert"), "tensor"),
        P(("dp", "expert"), "tensor"),
        P(("dp", "expert"), None),
        P(("dp", "expert"), None),
        P(("dp", "expert")),
        P(),
        P(),
        P("expert", None, ("dp", "tensor")),
        P("expert", None, ("dp", "tensor")),
        P("expert", ("dp", "tensor"), None),
    )
    out_specs = (
        P(("dp", "expert"), "tensor"),
        P(("dp", "expert"), None),
        P("expert", None, ("dp", "tensor")),
        P("expert", None, ("dp", "tensor")),
        P("expert", ("dp", "tensor"), None),
    )
    return jax.shard_map(shards, mesh=mesh, in_specs=in_specs, out_specs=out_specs, check_vma=False)
```

profile of v0, /device:TPU:7, one launch (start us, length us, event | category | flops | bytes accessed | tf_op | source)
XLA Modules:
  0.0 338.9 jit_solution(15449962634105801400)
XLA Ops:
  9.7 1.0 fusion.53
  13.2 1.3 fusion.15
  15.4 35.8 %all_to_all.15 = bf16[16,6,3584]{2,1,0:T(8,128)(2,1)S(1)} all-to-all(bf16[16,6,3584]{2,1,0:T(8,128)(2,1)S(1)} %copy.32), channel_id=1, replica_groups=mesh['dp'=8,'expert'=16,'tensor'=2] {'expert'}, dimensions={0} | all-to-all | bytes 1376256 | tf_op jit(solution)/shard_map/all_to_all | solution.py:55
  52.8 37.7 %all_to_all.16 = bf16[16,5,3584]{2,1,0:T(8,128)(2,1)S(1)} all-to-all(bf16[16,5,3584]{2,1,0:T(8,128)(2,1)S(1)} %copy.33), channel_id=1, replica_groups=mesh['dp'=8,'expert'=16,'tensor'=2] {'expert'}, dimensions={0} | all-to-all | bytes 1146880 | tf_op jit(solution)/shard_map/all_to_all | solution.py:59
  92.2 2.3 reshape_squeeze.17
  94.6 33.8 %all-gather.3.cloned.1.call-done = bf16[1408,3584]{1,0:T(8,128)(2,1)} async-done(((bf16[88,3584]{1,0:T(8,128)(2,1)}), bf16[1408,3584]{1,0:T(8,128)(2,1)}) %all-gather.3.cloned.1.call-update) | async-done | bytes 10092560 | tf_op jit(solution)/shard_map/all_gather | solution.py:61
  128.4 2.4 slice-done.3
  130.9 4.3 %fusion.23 = f32[704,256]{1,0:T(8,128)S(1)} fusion(bf16[2,3584,128]{2,1,0:T(8,128)(2,1)} %bitcast.117, bf16[2,3584,128]{2,1,0:T(8,128)(2,1)S(1)} %bitcast.115, bf16[1408,3584]{1,0:T(8,128)(2,1)} %all-gather.3.cloned.1.call-done), kind=kOutput, calls=%fused_computation.28 | convolution fusion | flops 1295515648 | bytes 9437184 | tf_op jit(solution)/shard_map/dot_general | solution.py:73
  135.3 1.3 copy-done.2
  137.6 2.3 fusion.33
  139.9 53.8 %all-gather.5.cloned.1.call-done = bf16[1408,3584]{1,0:T(8,128)(2,1)} async-done(((bf16[88,3584]{1,0:T(8,128)(2,1)}), bf16[1408,3584]{1,0:T(8,128)(2,1)}) %all-gather.5.cloned.1.call-update) | async-done | bytes 10092560 | tf_op jit(solution)/shard_map/all_gather | solution.py:63
  193.7 6.8 %multiply_convert_fusion.2 = (bf16[704,128]{1,0:T(8,128)(2,1)S(1)}, bf16[704,128]{1,0:T(8,128)(2,1)S(1)}, bf16[704,128]{1,0:T(8,128)(2,1)S(1)}, f32[704,128]{1,0:T(8,128)S(1)}) fusion(f32[704,256]{1,0:T(8,128)} %fusion.33, f32[704]{0:T(1024)S(1)} %reshape.266, bf16[2,704,3584]{2,1,0:T(8,128)(2,1)} %bitcast.92, bf16[128,2,3584]{2,1,0:T(2,128)(2,1)S(1)} %copy-done.4), kind=kOutput, calls=%fused_computation.65 | convolution fusion | flops 1293287424 | bytes 13552384 | tf_op jit(solution)/shard_map/tsf,htf->sh/dot_general | solution.py:77
  201.2 9.4 %convolution_convert_fusion = bf16[2,3584,704]{1,2,0:T(8,128)(2,1)} fusion(bf16[2,3584,128]{2,1,0:T(8,128)(2,1)S(1)} %broadcast_in_dim.8, bf16[2,3584,128]{2,1,0:T(8,128)(2,1)} %bitcast.114, bf16[2,3584,128]{2,1,0:T(8,128)(2,1)} %bitcast.118, bf16[704,128]{1,0:T(8,128)(2,1)S(1)} %bitcast.101, bf16[704,128]{1,0:T(8,128)(2,1)S(1)} %get-tuple-element.80, ...), kind=kOutput, calls=%fused_computation | convolution fusion | flops 3898720256 | bytes 16138240 | tf_op jit(solution)/shard_map/sk,tfk->tsf/dot_general | solution.py:119
  210.7 3.4 %fusion.9 = bf16[128,3584]{1,0:T(8,128)(2,1)S(1)} fusion(bf16[1408,3584]{1,0:T(8,128)(2,1)} %all-gather.5.cloned.1.call-done, bf16[704,128]{1,0:T(8,128)(2,1)S(1)} %get-tuple-element.81, f32[704]{0:T(1024)S(1)} %reshape.266), kind=kOutput, calls=%fused_computation.11 | convolution fusion | flops 646651904 | bytes 6146816 | tf_op jit(solution)/shard_map/dot_general | solution.py:90
  214.1 3.6 %fusion.12 = bf16[128,3584]{1,0:T(8,128)(2,1)S(1)} fusion(bf16[1408,3584]{1,0:T(8,128)(2,1)} %all-gather.5.cloned.1.call-done, bf16[704,128]{1,0:T(8,128)(2,1)S(1)} %get-tuple-element.81, f32[704]{0:T(1024)S(1)} %reshape.266), kind=kOutput, calls=%fused_computation.12 | convolution fusion | flops 646651904 | bytes 6146816 | tf_op jit(solution)/shard_map/dot_general | solution.py:90
  217.7 4.5 %convolution_convert_fusion.2 = bf16[3584,128]{1,0:T(8,128)(2,1)S(1)} fusion(bf16[704,128]{1,0:T(8,128)(2,1)S(1)} %get-tuple-element.80, bf16[1408,3584]{1,0:T(8,128)(2,1)} %all-gather.3.cloned.1.call-done), kind=kOutput, calls=%fused_computation.13 | convolution fusion | flops 646381568 | bytes 6144000 | tf_op jit(solution)/shard_map/dot_general | solution.py:104
  222.3 1.7 convolution_convert_fusion.3
  224.0 1.7 convolution_convert_fusion.4
  225.7 1.7 convolution_convert_fusion.5
  227.4 1.4 pad_maximum_fusion.3
  228.8 2.1 pad_maximum_fusion.1
  230.9 59.5 %reduce-scatter.2.cloned.1.call-done = bf16[88,3584]{1,0:T(8,128)(2,1)} async-done(((bf16[1408,3584]{1,0:T(8,128)(2,1)}), bf16[88,3584]{1,0:T(8,128)(2,1)}) %reduce-scatter.2.cloned.1.call-update) | async-done | bytes 630800 | tf_op jit(solution)/shard_map/reduce_scatter | solution.py:121
  292.0 1.1 slice.189
  294.6 35.8 %all_to_all.17 = bf16[16,6,3584]{2,1,0:T(8,128)(2,1)S(1)} all-to-all(bf16[16,6,3584]{2,1,0:T(8,128)(2,1)S(1)} %fusion.42), channel_id=1, replica_groups=mesh['dp'=8,'expert'=16,'tensor'=2] {'expert'}, dimensions={0} | all-to-all | bytes 1376256 | tf_op jit(solution)/shard_map/all_to_all | solution.py:138
  (77 shorter events, 16.2 us)
Async XLA Ops:
  7.2 7.4 %copy-start = (bf16[8,8]{1,0:T(8,128)(2,1)S(1)}, bf16[8,8]{1,0:T(8,128)(2,1)}, u32[]{:S(2)}) copy-start(bf16[8,8]{1,0:T(8,128)(2,1)} %param.22) | copy-start | bytes 388
  7.2 121.2 %all-gather.3.cloned.1.call-start = ((), (), s32[]{:S(2)}) async-start(), calls=%async_computation.4 | async-start | bytes 10723328 | tf_op jit(solution)/shard_map/all_gather | solution.py:61
  12.3 2.3 copy-start.5
  52.4 141.3 %all-gather.5.cloned.1.call-start = ((), (), s32[]{:S(2)}) async-start(), calls=%async_computation.5 | async-start | bytes 10723328 | tf_op jit(solution)/shard_map/all_gather | solution.py:63
  90.5 1.7 copy-start.3
  91.6 198.7 %reduce-scatter.2.cloned.1.call-start = ((), (), s32[]{:S(2)}) async-start(), calls=%async_computation.6 | async-start | bytes 10723328 | tf_op jit(solution)/shard_map/reduce_scatter | solution.py:121
  94.6 36.4 %copy-start.6 = (bf16[1,7168,128]{2,1,0:T(8,128)(2,1)S(1)}, bf16[1,7168,128]{2,1,0:T(8,128)(2,1)}, u32[]{:S(2)}) copy-start(bf16[1,7168,128]{2,1,0:T(8,128)(2,1)} %param.28) | copy-start | bytes 5505028
  128.4 2.4 slice-start.3
  130.9 5.6 %copy-start.2 = (bf16[1408,3584]{1,0:T(8,128)(2,1)S(1)}, bf16[1408,3584]{1,0:T(8,128)(2,1)}, u32[]{:S(2)}) copy-start(bf16[1408,3584]{1,0:T(8,128)(2,1)} %all-gather.3.cloned.1.call-done) | copy-start | bytes 30277636
  130.9 6.1 %copy-start.7 = (bf16[1,7168,128]{2,1,0:T(8,128)(2,1)S(1)}, bf16[1,7168,128]{2,1,0:T(8,128)(2,1)}, u32[]{:S(2)}) copy-start(bf16[1,7168,128]{2,1,0:T(8,128)(2,1)} %param.28) | copy-start | bytes 5505028
  130.9 6.6 %copy-start.8 = (bf16[1,7168,128]{2,1,0:T(8,128)(2,1)S(1)}, bf16[1,7168,128]{2,1,0:T(8,128)(2,1)}, u32[]{:S(2)}) copy-start(bf16[1,7168,128]{2,1,0:T(8,128)(2,1)} %param.27) | copy-start | bytes 5505028
  137.6 56.2 %copy-start.4 = (bf16[128,2,3584]{2,1,0:T(2,128)(2,1)S(1)}, bf16[128,2,3584]{2,1,0:T(2,128)(2,1)}, u32[]{:S(2)}) copy-start(bf16[128,2,3584]{2,1,0:T(2,128)(2,1)} %reshape_squeeze.17) | copy-start | bytes 5505028
  214.1 8.1 %slice-start = ((s8[10092544]{0:T(1024)(128)(4,1)}), s8[4194304]{0:T(1024)(128)(4,1)S(1)}, s32[]{:S(2)}) async-start(s8[10092544]{0:T(1024)(128)(4,1)} %bitcast.93), calls=%async_computation.7 | async-start | bytes 8388608
  214.1 8.1 %slice-start.1 = ((s8[10092544]{0:T(1024)(128)(4,1)}), s8[4194304]{0:T(1024)(128)(4,1)S(1)}, s32[]{:S(2)}) async-start(s8[10092544]{0:T(1024)(128)(4,1)} %bitcast.93), calls=%async_computation.8 | async-start | bytes 8388608
  217.7 4.5 %slice-start.2 = ((s8[10092544]{0:T(1024)(128)(4,1)}), s8[1703936]{0:T(1024)(128)(4,1)S(1)}, s32[]{:S(2)}) async-start(s8[10092544]{0:T(1024)(128)(4,1)} %bitcast.93), calls=%async_computation.9 | async-start | bytes 3407872
  291.1 2.4 collective-permute-start
  294.2 38.1 %copy-start.1 = (bf16[8,8]{1,0:T(8,128)(2,1)S(1)}, bf16[8,8]{1,0:T(8,128)(2,1)}, u32[]{:S(2)}) copy-start(bf16[8,8]{1,0:T(8,128)(2,1)} %param.22) | copy-start | bytes 388
Sparse Core Ops, SparseCore 0:
  52.6 75.7 all-gather.2
  130.8 62.8 all-gather.4
  210.8 79.4 reduce-scatter.1
where the time goes:
time: 340 us; the launch traced here: 339 us
  waiting for transfers between devices  147 us (43%)
  blocking collectives  109 us (32%)
  matrix products  43.9 us (13%)
  between operations  14.1 us (4%)
  local copies, waits for them, and re-layouts  12.2 us (4%)
  other arithmetic  11.1 us (3%)
    reduce_scatter x1, waiting for transfers between devices, shards(): lax.psum_scatter(product, ('tensor', 'dp'), scatter_dimension=0, tiled=True)  59.5 us
    all_gather x1, waiting for transfers between devices, shards(): g_cot = lax.all_gather(cot_rows, ('tensor', 'dp'), axis=0, tiled=True)  53.8 us
    all_to_all x1, blocking collectives, shards(): lax.all_to_all(cot_pack, 'expert', split_axis=0, concat_axis=0, tiled=True)  37.7 us
    all_to_all x1, blocking collectives, shards(): lax.all_to_all(tok_pack, 'expert', split_axis=0, concat_axis=0, tiled=True)  35.8 us
    all_to_all x1, blocking collectives, shards(): lax.all_to_all(back_pack, 'expert', split_axis=0, concat_axis=0, tiled=True)  35.8 us
    all_gather x1, waiting for transfers between devices, shards(): g_tok = lax.all_gather(tok_rows, ('tensor', 'dp'), axis=0, tiled=True)  33.8 us
    dot_general x1, matrix products, shards(): jnp.einsum('sk,tfk->tsf', lhs, w_out, preferred_element_type=f32)  9.44 us
    dot_general x2, matrix products, shards(): jnp.dot(weighted.T, g_cot[t], preferred_element_type=f32).astype(bf16)  7 us
  transfers between devices with their start and end apart: 4, of which 4 were waited for; matrix products, arithmetic and copies ran while one was open for 9% of the time, Pallas kernels for 0%

commit v1 on v0

--- a/solution.py
+++ b/solution.py
@@ -60,7 +60,12 @@
     cot_rows = jnp.concatenate([arrived_cot.reshape(slots, features), extra])
     g_tok = lax.all_gather(tok_rows, ("tensor", "dp"), axis=0, tiled=True)
     g_tok = g_tok.reshape(tensor_size, all_rows, features)
-    g_cot = lax.all_gather(cot_rows, ("tensor", "dp"), axis=0, tiled=True)
+    g_cot = jnp.concatenate(
+        lax.all_to_all(
+            jnp.stack([cot_rows] * lax.axis_size(("tensor", "dp"))), ("tensor", "dp"), 0, 0
+        ),
+        axis=0,
+    )
     g_cot = g_cot.reshape(tensor_size, all_rows, features)
     slot_prob = g_tok[0].reshape(dp_size, chunk, features)[:, slots, :chunk].reshape(all_rows)
     wg = w_gate[0].reshape(tensor_size, features, -1)

time: 340 us -> 403 us (1.19)
  waiting for transfers between devices: 147 us -> 193 us
  local copies, waits for them, and re-layouts: 12.2 us -> 22.3 us
  starting transfers between devices: 1.02 us -> 11 us
    all_gather x1, waiting for transfers between devices: 33.8 us -> 91.9 us  [shards(): g_tok = lax.all_gather(tok_rows, ('tensor', 'dp'), axis=0, tiled=True)]
    all_gather x1 -> x0, waiting for transfers between devices: 53.8 us -> none  [shards(): g_cot = lax.all_gather(cot_rows, ('tensor', 'dp'), axis=0, tiled=True)]
    all_to_all x0 -> x1, waiting for transfers between devices: none -> 42.1 us  [shards(): lax.all_to_all(jnp.stack([cot_rows] * lax.axis_size(('tensor', 'dp'))), (...]
    all_to_all x0 -> x1, starting transfers between devices: none -> 9.7 us  [shards(): lax.all_to_all(jnp.stack([cot_rows] * lax.axis_size(('tensor', 'dp'))), (...]
    slice x0 -> x1, local copies, waits for them, and re-layouts: none -> 6.92 us  [shards(): g_cot[t]]
    another operation x3 -> x4, local copies, waits for them, and re-layouts: 0.28 us -> 4.75 us  [the longest x1 4.46 us: shards(): jnp.stack([cot_rows] * lax.axis_size(('tensor', 'dp')))]
  transfers between devices with their start and end apart: 4 -> 4, of which waited for: 4 -> 3; matrix products, arithmetic and copies ran while one was open for 9% -> 10% of each run, Pallas kernels for 0% -> 0%
where the time goes in v1:
time: 403 us; the launch traced here: 402 us
  waiting for transfers between devices  193 us (48%)
  blocking collectives  109 us (27%)
  matrix products  41.5 us (10%)
  local copies, waits for them, and re-layouts  22.3 us (6%)
  between operations  14.4 us (4%)
  other arithmetic  11.2 us (3%)
  starting transfers between devices  11 us (3%)
    all_gather x1, waiting for transfers between devices, shards(): g_tok = lax.all_gather(tok_rows, ('tensor', 'dp'), axis=0, tiled=True)  91.9 us
    reduce_scatter x1, waiting for transfers between devices, shards(): lax.psum_scatter(product, ('tensor', 'dp'), scatter_dimension=0, tiled=True)  58.7 us
    all_to_all x1, waiting for transfers between devices, shards(): lax.all_to_all(jnp.stack([cot_rows] * lax.axis_size(('tensor', 'dp'))), (...  42.1 us
    all_to_all x1, blocking collectives, shards(): lax.all_to_all(cot_pack, 'expert', split_axis=0, concat_axis=0, tiled=True)  37.8 us
    all_to_all x1, blocking collectives, shards(): lax.all_to_all(back_pack, 'expert', split_axis=0, concat_axis=0, tiled=True)  35.7 us
    all_to_all x1, blocking collectives, shards(): lax.all_to_all(tok_pack, 'expert', split_axis=0, concat_axis=0, tiled=True)  35.6 us
    all_to_all x1, starting transfers between devices, shards(): lax.all_to_all(jnp.stack([cot_rows] * lax.axis_size(('tensor', 'dp'))), (...  9.7 us
    dot_general x1, matrix products, shards(): jnp.einsum('sk,tfk->tsf', lhs, w_out, preferred_element_type=f32)  9.44 us
  transfers between devices with their start and end apart: 4, of which 3 were waited for; matrix products, arithmetic and copies ran while one was open for 10% of the time, Pallas kernels for 0%

profile of v1, /device:TPU:7, one launch (start us, length us, event | category | flops | bytes accessed | tf_op | source)
XLA Modules:
  0.0 402.2 jit_solution(14571382855347355605)
XLA Ops:
  13.2 1.3 fusion.5
  15.4 35.6 %all_to_all.20 = bf16[16,6,3584]{2,1,0:T(8,128)(2,1)S(1)} all-to-all(bf16[16,6,3584]{2,1,0:T(8,128)(2,1)S(1)} %copy.32), channel_id=1, replica_groups=mesh['dp'=8,'expert'=16,'tensor'=2] {'expert'}, dimensions={0} | all-to-all | bytes 1376256 | tf_op jit(solution)/shard_map/all_to_all | solution.py:55
  52.7 37.8 %all_to_all.21 = bf16[16,5,3584]{2,1,0:T(8,128)(2,1)S(1)} all-to-all(bf16[16,5,3584]{2,1,0:T(8,128)(2,1)S(1)} %copy.33), channel_id=1, replica_groups=mesh['dp'=8,'expert'=16,'tensor'=2] {'expert'}, dimensions={0} | all-to-all | bytes 1146880 | tf_op jit(solution)/shard_map/all_to_all | solution.py:59
  90.7 4.5 %stack.11 = bf16[16,88,3584]{2,1,0:T(8,128)(2,1)} broadcast(bf16[88,3584]{1,0:T(8,128)(2,1)S(1)} %concatenate.45), dimensions={1,2} | broadcast | bytes 10723328 | tf_op jit(solution)/shard_map/stack | solution.py:65
  95.2 9.7 %all-to-all-start.2 = ((bf16[16,88,3584]{2,1,0:T(8,128)(2,1)}), bf16[16,88,3584]{2,1,0:T(8,128)(2,1)}, u32[]{:S(2)}, u32[]{:S(2)}) async-start(bf16[16,88,3584]{2,1,0:T(8,128)(2,1)} %stack.11), calls=%async_computation.2 | async-start | bytes 20185088 | tf_op jit(solution)/shard_map/all_to_all | solution.py:64
  104.9 2.3 reshape_squeeze.17
  107.3 91.9 %all-gather.2.cloned.1.call-done = bf16[1408,3584]{1,0:T(8,128)(2,1)} async-done(((bf16[88,3584]{1,0:T(8,128)(2,1)}), bf16[1408,3584]{1,0:T(8,128)(2,1)}) %all-gather.2.cloned.1.call-update) | async-done | bytes 10092560 | tf_op jit(solution)/shard_map/all_gather | solution.py:61
  199.2 2.4 slice-done.3
  201.8 4.3 %fusion.13 = f32[704,256]{1,0:T(8,128)S(1)} fusion(bf16[2,3584,128]{2,1,0:T(8,128)(2,1)} %bitcast.122, bf16[2,3584,128]{2,1,0:T(8,128)(2,1)S(1)} %bitcast.120, bf16[1408,3584]{1,0:T(8,128)(2,1)} %all-gather.2.cloned.1.call-done), kind=kOutput, calls=%fused_computation.24 | convolution fusion | flops 1295515648 | bytes 9437184 | tf_op jit(solution)/shard_map/dot_general | solution.py:78
  206.1 1.3 copy-done.2
  208.4 2.3 fusion.23
  210.7 42.1 %all-to-all-done.2 = bf16[16,88,3584]{2,1,0:T(8,128)(2,1)} async-done(((bf16[16,88,3584]{2,1,0:T(8,128)(2,1)}), bf16[16,88,3584]{2,1,0:T(8,128)(2,1)}, u32[]{:S(2)}, u32[]{:S(2)}) %all-to-all-start.2) | async-done | bytes 10092576 | tf_op jit(solution)/shard_map/all_to_all | solution.py:64
  252.9 6.8 %multiply_convert_fusion.2 = (bf16[704,128]{1,0:T(8,128)(2,1)S(1)}, bf16[704,128]{1,0:T(8,128)(2,1)S(1)}, bf16[704,128]{1,0:T(8,128)(2,1)S(1)}, f32[704,128]{1,0:T(8,128)S(1)}) fusion(f32[704,256]{1,0:T(8,128)} %fusion.23, f32[704]{0:T(1024)S(1)} %reshape.264, bf16[2,704,3584]{2,1,0:T(8,128)(2,1)} %bitcast.24, bf16[128,2,3584]{2,1,0:T(2,128)(2,1)S(1)} %copy-done.4), kind=kOutput, calls=%fused_computation.61 | convolution fusion | flops 1293287424 | bytes 13552384 | tf_op jit(solution)/shard_map/tsf,htf->sh/dot_general | solution.py:82
  260.4 9.4 %convolution_convert_fusion = bf16[2,3584,704]{1,2,0:T(8,128)(2,1)} fusion(bf16[2,3584,128]{2,1,0:T(8,128)(2,1)S(1)} %broadcast_in_dim.8, bf16[2,3584,128]{2,1,0:T(8,128)(2,1)} %bitcast.119, bf16[2,3584,128]{2,1,0:T(8,128)(2,1)} %bitcast.123, bf16[704,128]{1,0:T(8,128)(2,1)S(1)} %bitcast.106, bf16[704,128]{1,0:T(8,128)(2,1)S(1)} %get-tuple-element.82, ...), kind=kOutput, calls=%fused_computation | convolution fusion | flops 3898720256 | bytes 16138240 | tf_op jit(solution)/shard_map/sk,tfk->tsf/dot_general | solution.py:124
  269.8 6.9 %fusion.80 = (bf16[8,88,3584]{2,1,0:T(8,128)(2,1)}, bf16[8,88,3584]{2,1,0:T(8,128)(2,1)S(1)}) fusion(bf16[16,88,3584]{2,1,0:T(8,128)(2,1)} %all-to-all-done.2), kind=kLoop, calls=%fused_computation.117 | loop fusion | bytes 20185088 | tf_op jit(solution)/shard_map/slice | solution.py:95
  276.8 3.4 convolution_convert_fusion.3
  281.2 4.6 %convolution_convert_fusion.4 = bf16[3584,128]{1,0:T(8,128)(2,1)S(1)} fusion(bf16[704,128]{1,0:T(8,128)(2,1)S(1)} %get-tuple-element.82, bf16[1408,3584]{1,0:T(8,128)(2,1)} %all-gather.2.cloned.1.call-done), kind=kOutput, calls=%fused_computation.9 | convolution fusion | flops 646381568 | bytes 6144000 | tf_op jit(solution)/shard_map/dot_general | solution.py:109
  285.9 1.7 convolution_convert_fusion.5
  287.6 1.7 convolution_convert_fusion.6
  289.3 1.7 convolution_convert_fusion.7
  291.0 1.4 pad_maximum_fusion.3
  292.4 2.1 pad_maximum_fusion.1
  294.5 58.7 %reduce-scatter.2.cloned.1.call-done = bf16[88,3584]{1,0:T(8,128)(2,1)} async-done(((bf16[1408,3584]{1,0:T(8,128)(2,1)}), bf16[88,3584]{1,0:T(8,128)(2,1)}) %reduce-scatter.2.cloned.1.call-update) | async-done | bytes 630800 | tf_op jit(solution)/shard_map/reduce_scatter | solution.py:126
  357.6 35.7 %all_to_all.22 = bf16[16,6,3584]{2,1,0:T(8,128)(2,1)S(1)} all-to-all(bf16[16,6,3584]{2,1,0:T(8,128)(2,1)S(1)} %fusion.32), channel_id=1, replica_groups=mesh['dp'=8,'expert'=16,'tensor'=2] {'expert'}, dimensions={0} | all-to-all | bytes 1376256 | tf_op jit(solution)/shard_map/all_to_all | solution.py:143
  (78 shorter events, 18.1 us)
Async XLA Ops:
  7.2 7.4 %copy-start = (bf16[8,8]{1,0:T(8,128)(2,1)S(1)}, bf16[8,8]{1,0:T(8,128)(2,1)}, u32[]{:S(2)}) copy-start(bf16[8,8]{1,0:T(8,128)(2,1)} %param.22) | copy-start | bytes 388
  7.2 7.4 %copy-start.5 = (s32[8,8]{1,0:T(8,128)S(1)}, s32[8,8]{1,0:T(8,128)}, u32[]{:S(2)}) copy-start(s32[8,8]{1,0:T(8,128)} %param.23) | copy-start | bytes 772
  7.2 192.0 %all-gather.2.cloned.1.call-start = ((), (), s32[]{:S(2)}) async-start(), calls=%async_computation.5 | async-start | bytes 10723328 | tf_op jit(solution)/shard_map/all_gather | solution.py:61
  95.2 9.7 %copy-start.3 = (bf16[1,128,7168]{2,1,0:T(8,128)(2,1)S(1)}, bf16[1,128,7168]{2,1,0:T(8,128)(2,1)}, u32[]{:S(2)}) copy-start(bf16[1,128,7168]{2,1,0:T(8,128)(2,1)} %param.29) | copy-start | bytes 5505028
  95.2 157.7 %all-to-all-start.2 = ((bf16[16,88,3584]{2,1,0:T(8,128)(2,1)}), bf16[16,88,3584]{2,1,0:T(8,128)(2,1)}, u32[]{:S(2)}, u32[]{:S(2)}) async-start(bf16[16,88,3584]{2,1,0:T(8,128)(2,1)} %stack.11), calls=%async_computation.2 | async-start | bytes 20185088 | tf_op jit(solution)/shard_map/all_to_all | solution.py:64
  104.9 248.3 %reduce-scatter.2.cloned.1.call-start = ((), (), s32[]{:S(2)}) async-start(), calls=%async_computation.6 | async-start | bytes 10723328 | tf_op jit(solution)/shard_map/reduce_scatter | solution.py:126
  107.3 94.5 %copy-start.6 = (bf16[1,7168,128]{2,1,0:T(8,128)(2,1)S(1)}, bf16[1,7168,128]{2,1,0:T(8,128)(2,1)}, u32[]{:S(2)}) copy-start(bf16[1,7168,128]{2,1,0:T(8,128)(2,1)} %param.28) | copy-start | bytes 5505028
  199.2 2.4 slice-start.3
  201.7 5.6 %copy-start.2 = (bf16[1408,3584]{1,0:T(8,128)(2,1)S(1)}, bf16[1408,3584]{1,0:T(8,128)(2,1)}, u32[]{:S(2)}) copy-start(bf16[1408,3584]{1,0:T(8,128)(2,1)} %all-gather.2.cloned.1.call-done) | copy-start | bytes 30277636
  201.8 6.1 %copy-start.7 = (bf16[1,7168,128]{2,1,0:T(8,128)(2,1)S(1)}, bf16[1,7168,128]{2,1,0:T(8,128)(2,1)}, u32[]{:S(2)}) copy-start(bf16[1,7168,128]{2,1,0:T(8,128)(2,1)} %param.28) | copy-start | bytes 5505028
  201.8 6.6 %copy-start.8 = (bf16[1,7168,128]{2,1,0:T(8,128)(2,1)S(1)}, bf16[1,7168,128]{2,1,0:T(8,128)(2,1)}, u32[]{:S(2)}) copy-start(bf16[1,7168,128]{2,1,0:T(8,128)(2,1)} %param.27) | copy-start | bytes 5505028
  208.4 44.5 %copy-start.4 = (bf16[128,2,3584]{2,1,0:T(2,128)(2,1)S(1)}, bf16[128,2,3584]{2,1,0:T(2,128)(2,1)}, u32[]{:S(2)}) copy-start(bf16[128,2,3584]{2,1,0:T(2,128)(2,1)} %reshape_squeeze.17) | copy-start | bytes 5505028
  280.2 5.6 %slice-start = ((s8[10092544]{0:T(1024)(128)(4,1)}), s8[4194304]{0:T(1024)(128)(4,1)S(1)}, s32[]{:S(2)}) async-start(s8[10092544]{0:T(1024)(128)(4,1)} %bitcast.98), calls=%async_computation.7 | async-start | bytes 8388608
  280.2 5.6 %slice-start.1 = ((s8[10092544]{0:T(1024)(128)(4,1)}), s8[4194304]{0:T(1024)(128)(4,1)S(1)}, s32[]{:S(2)}) async-start(s8[10092544]{0:T(1024)(128)(4,1)} %bitcast.98), calls=%async_computation.8 | async-start | bytes 8388608
  281.2 4.6 %slice-start.2 = ((s8[10092544]{0:T(1024)(128)(4,1)}), s8[1703936]{0:T(1024)(128)(4,1)S(1)}, s32[]{:S(2)}) async-start(s8[10092544]{0:T(1024)(128)(4,1)} %bitcast.98), calls=%async_computation.9 | async-start | bytes 3407872
  353.9 2.6 collective-permute-start
  356.2 39.1 %copy-start.1 = (bf16[8,8]{1,0:T(8,128)(2,1)S(1)}, bf16[8,8]{1,0:T(8,128)(2,1)}, u32[]{:S(2)}) copy-start(bf16[8,8]{1,0:T(8,128)(2,1)} %param.22) | copy-start | bytes 388
Sparse Core Ops, SparseCore 0:
  52.4 146.7 all-gather.1
  270.0 83.1 reduce-scatter.1
